TPU v7x, 512 devices: a whole 4x4x16 slice. The times are simulated.
512 devices in a mesh: ctx: 16 (over z), ep: 32 (over y, x, core).
Axes of the slice: x: 4, y: 4, z: 16, core: 2. Of those that a mesh axis runs over, the one named last changes fastest.
Arguments:
- query_act: bfloat16 [2048, 8192], P('ctx', 'ep'), may hold values from -6 to 6
- key_act: bfloat16 [2048, 8192], P('ctx', 'ep'), may hold values from -6 to 6
- value_act: bfloat16 [2048, 8192], P('ctx', 'ep'), may hold values from -6 to 6
- state_init: float32 [64, 128, 128], P('ep'), may hold values from -128 to 128
- head_gain: float32 [8192], P('ep'), may hold values from 0.25 to 1.75
- out_weight: bfloat16 [8192, 3072], P('ctx', 'ep'), may hold values from -0.0625 to 0.0625
- stream_in: bfloat16 [2048, 3072], P('ctx', 'ep'), may hold values from -150 to 150
- model_gain: float32 [3072], replicated, may hold values from 0.25 to 1.75
- expert_ids: int32 [2048, 2], P('ctx'), may hold values from 0 to 15, as said below
- expert_slots: int32 [2048, 2], P('ctx'), may hold values from 0 to 19, as said below
- route_gates: float32 [2048, 2], P('ctx'), may hold values from 0.2 to 1
- gate_weight: bfloat16 [32, 3072, 3072], P('ep', 'ctx'), may hold values from -0.109375 to 0.109375
- up_weight: bfloat16 [32, 3072, 3072], P('ep', 'ctx'), may hold values from -0.109375 to 0.109375
- down_weight: bfloat16 [32, 3072, 3072], P('ep', 'ctx'), may hold values from -0.078125 to 0.078125
- out_grad: bfloat16 [2048, 3072], P('ctx', 'ep'), may hold values from -6 to 6
Outputs:
- layer_out: bfloat16 [2048, 3072], P('ctx', 'ep')
- grad_query: bfloat16 [2048, 8192], P('ctx', 'ep')
- grad_key: bfloat16 [2048, 8192], P('ctx', 'ep')
- grad_value: bfloat16 [2048, 8192], P('ctx', 'ep')
- grad_state: float32 [64, 128, 128], P('ep')
- grad_stream: bfloat16 [2048, 3072], P('ctx', 'ep')
Inputs may be any that keep to these rules, and one draw needn't show every extreme that they name: `expert_ids`: within each block of 128 tokens a token's two experts differ; the tokens naming expert e hold the slots 0 to n - 1 of e once each, n being their number; no expert is named by more than 20 tokens of a block, and in every block some expert by exactly 20. `expert_slots`: see expert_ids.
All inputs are finite; a program needn't handle non-finite values.
Results may differ from a plain program's by a relative error of at most 0.02.
Values may be sent and summed in bfloat16 or wider, within the bound.
No kernel may reach another device: no remote copies, remote signals or barrier semaphores. Data moves between devices by JAX's collectives and lax.ppermute only.
A program may use at most 64 MiB of HBM per device.

v0:
```python
import jax
import jax.numpy as jnp
from jax import lax
from jax.sharding import PartitionSpec as P


def carried_in(value, axis, join, neutral, backward):
    count = lax.axis_size(axis)
    place = lax.axis_index(axis)
    ahead = count - 1 - place if backward else place
    gathered = lax.all_gather(value.astype(jnp.bfloat16), axis)
    state = jnp.zeros_like(value) + jnp.asarray(neutral, value.dtype)

    def one(turn, state):
        source = count - 1 - turn if backward else turn
        return join(state, lax.dynamic_index_in_dim(gathered, source, 0, False).astype(value.dtype))

    return lax.fori_loop(0, ahead, one, state)


def head_normalize(attended, gain):
    factor = lax.rsqrt(jnp.mean(attended * attended, -1, keepdims=True) + 1e-06)
    return attended * factor * gain


def add_states(earlier, later_one):
    return earlier + later_one


def contract_last(left, right):
    return lax.dot_general(
        left, right, (((1,), (1,)), ((), ())), preferred_element_type=jnp.float32
    )


def local(
    query_act,
    key_act,
    value_act,
    state_init,
    head_gain,
    out_weight,
    stream_in,
    model_gain,
    expert_ids,
    expert_slots,
    route_gates,
    gate_weight,
    up_weight,
    down_weight,
    out_grad,
):
    f32 = jnp.float32
    high = lax.Precision.HIGHEST
    ep_count = lax.axis_size("ep")
    expert_count = ep_count // 2
    my_ep = lax.axis_index("ep")
    tokens_here = query_act.shape[0]
    head_count = state_init.shape[0]
    head_size = state_init.shape[1]
    model_width = model_gain.shape[0]
    columns = stream_in.shape[1]
    capacity = 5 * tokens_here // (2 * expert_count)
    query3 = query_act.reshape(tokens_here, head_count, head_size)
    key3 = key_act.reshape(tokens_here, head_count, head_size)
    value3 = value_act.reshape(tokens_here, head_count, head_size)
    kv_own = jnp.einsum("thd,the->hde", key3, value3, preferred_element_type=f32)
    zero_state = jnp.zeros_like(kv_own)
    before = carried_in(kv_own, "ctx", add_states, zero_state, False)
    prefix = state_init + before
    causal = jnp.arange(tokens_here)[:, None] >= jnp.arange(tokens_here)[None, :]
    scores = jnp.einsum("thd,shd->hts", query3, key3, preferred_element_type=f32)
    scores_bf = jnp.where(causal[None], scores, 0.0).astype(jnp.bfloat16)
    inside = jnp.einsum("hts,she->the", scores_bf, value3, preferred_element_type=f32)
    from_state = jnp.einsum("thd,hde->the", query3.astype(f32), prefix, precision=high)
    attended = from_state + inside
    gain_heads = head_gain.reshape(head_count, head_size)
    normed_heads = (
        head_normalize(attended, gain_heads)
        .astype(jnp.bfloat16)
        .reshape(tokens_here, head_count * head_size)
    )
    w_cols = lax.all_gather(out_weight, "ctx", axis=0, tiled=True)
    attn_proj = jnp.dot(
        lax.all_gather(normed_heads, "ep", axis=1, tiled=True), w_cols, preferred_element_type=f32
    )
    stream = (stream_in.astype(f32) + attn_proj).astype(jnp.bfloat16)
    stream_f = stream.astype(f32)
    gain_cols = lax.dynamic_slice_in_dim(model_gain, my_ep * columns, columns, 0)
    dest_expert = jnp.arange(ep_count) % expert_count
    slot_iota = jnp.arange(capacity)
    hits = (expert_ids[:, :, None, None] == dest_expert[None, None, :, None]) & (
        expert_slots[:, :, None, None] == slot_iota[None, None, None, :]
    )
    hits_f = hits.astype(f32)
    dest_picks = jnp.sum(hits_f, 1).reshape(tokens_here, ep_count * capacity)
    dest_weights = jnp.sum(hits_f * route_gates[:, :, None, None], 1).reshape(
        tokens_here, ep_count * capacity
    )
    whole_rows = lax.all_gather(stream, "ep", axis=1, tiled=True).astype(f32)
    row_scale = lax.rsqrt(jnp.mean(whole_rows * whole_rows, -1, keepdims=True) + 1e-05)
    model_in = (whole_rows * row_scale * model_gain).astype(jnp.bfloat16)
    own_select = lax.dynamic_slice_in_dim(dest_picks, my_ep * capacity, capacity, 1).T.astype(
        jnp.bfloat16
    )
    expert_in = jnp.dot(own_select, model_in, preferred_element_type=f32).astype(jnp.bfloat16)
    w_gate = gate_weight[0]
    w_up = up_weight[0]
    w_down = down_weight[0]
    hidden_block = w_gate.shape[0]
    portion = lax.all_gather(expert_in, "ctx", axis=0, tiled=True)
    projected = jnp.concatenate([contract_last(portion, w_gate), contract_last(portion, w_up)], 1)
    pre_gate = projected[:, :hidden_block]
    pre_up = projected[:, hidden_block:]
    gate_sig = jax.nn.sigmoid(pre_gate)
    activated = (pre_gate * gate_sig * pre_up).astype(jnp.bfloat16)
    half_out = lax.psum_scatter(
        jnp.dot(activated, w_down, preferred_element_type=f32).astype(jnp.bfloat16),
        "ctx",
        scatter_dimension=0,
        tiled=True,
    )
    returned = lax.all_to_all(half_out, "ep", split_axis=1, concat_axis=0, tiled=True)
    expert_mix = jnp.dot(dest_weights, returned.astype(f32), precision=high)
    layer_out = (stream_f + expert_mix).astype(jnp.bfloat16)
    grad_out = out_grad.astype(f32)
    grad_send = jnp.dot(dest_weights.T, grad_out, precision=high).astype(jnp.bfloat16)
    grad_in = lax.all_to_all(grad_send, "ep", split_axis=0, concat_axis=1, tiled=True)
    grad_act = contract_last(lax.all_gather(grad_in, "ctx", axis=0, tiled=True), w_down)
    grad_gate_pre = (grad_act * pre_up * gate_sig * (1.0 + pre_gate * (1.0 - gate_sig))).astype(
        jnp.bfloat16
    )
    grad_up_pre = (grad_act * pre_gate * gate_sig).astype(jnp.bfloat16)
    grad_half = lax.psum_scatter(
        (
            jnp.dot(grad_gate_pre, w_gate, preferred_element_type=f32)
            + jnp.dot(grad_up_pre, w_up, preferred_element_type=f32)
        ).astype(jnp.bfloat16),
        "ctx",
        scatter_dimension=0,
        tiled=True,
    )
    grad_back = lax.all_to_all(grad_half, "ep", split_axis=1, concat_axis=0, tiled=True)
    grad_model_in = jnp.dot(dest_picks, grad_back.astype(f32), precision=high)
    scaled_grad = grad_model_in * gain_cols
    inner_sum = lax.psum(jnp.sum(stream_f * scaled_grad, -1), "ep")
    grad_stream = (
        grad_out
        + row_scale * scaled_grad
        - stream_f * row_scale**3 * inner_sum[:, None] / model_width
    ).astype(jnp.bfloat16)
    w_rows = lax.all_to_all(w_cols, "ep", split_axis=0, concat_axis=1, tiled=True)
    grad_heads = contract_last(lax.all_gather(grad_stream, "ep", axis=1, tiled=True), w_rows)
    head_pull = jax.vjp(lambda value: head_normalize(value, gain_heads), attended)[1]
    grad_attended = head_pull(grad_heads.reshape(tokens_here, head_count, head_size))[0].astype(
        jnp.bfloat16
    )
    state_part = jnp.einsum("thd,the->hde", query3, grad_attended, preferred_element_type=f32)
    later_sum = carried_in(state_part, "ctx", add_states, zero_state, True)
    state_total = lax.psum(state_part.astype(jnp.bfloat16), "ctx").astype(jnp.float32)
    grad_scores = jnp.einsum("the,she->hts", grad_attended, value3, preferred_element_type=f32)
    grad_masked = jnp.where(causal[None], grad_scores, 0.0).astype(jnp.bfloat16)
    grad_att_f = grad_attended.astype(f32)
    grad_query = jnp.einsum("the,hde->thd", grad_att_f, prefix, precision=high) + jnp.einsum(
        "hts,shd->thd", grad_masked, key3, preferred_element_type=f32
    )
    grad_key = jnp.einsum(
        "the,hde->thd", value3.astype(f32), later_sum, precision=high
    ) + jnp.einsum("hts,thd->shd", grad_masked, query3, preferred_element_type=f32)
    grad_value = jnp.einsum(
        "thd,hde->the", key3.astype(f32), later_sum, precision=high
    ) + jnp.einsum("hts,the->she", scores_bf, grad_attended, preferred_element_type=f32)
    flat_shape = (tokens_here, head_count * head_size)
    return (
        layer_out,
        grad_query.astype(jnp.bfloat16).reshape(flat_shape),
        grad_key.astype(jnp.bfloat16).reshape(flat_shape),
        grad_value.astype(jnp.bfloat16).reshape(flat_shape),
        state_total,
        grad_stream,
    )


def solution(mesh):
    return jax.shard_map(
        local,
        mesh=mesh,
        in_specs=(
            P("ctx", "ep"),
            P("ctx", "ep"),
            P("ctx", "ep"),
            P("ep", None, None),
            P("ep"),
            P("ctx", "ep"),
            P("ctx", "ep"),
            P(),
            P("ctx", None),
            P("ctx", None),
            P("ctx", None),
            P("ep", "ctx", None),
            P("ep", "ctx", None),
            P("ep", "ctx", None),
            P("ctx", "ep"),
        ),
        out_specs=(
            P("ctx", "ep"),
            P("ctx", "ep"),
            P("ctx", "ep"),
            P("ctx", "ep"),
            P("ep", None, None),
            P("ctx", "ep"),
        ),
        check_vma=False,
    )
```

profile of v0, /device:TPU:2, one launch (start us, length us, event | category | flops | bytes accessed | tf_op | source)
XLA Modules:
  0.0 797.9 jit_solution(11163868636489932232)
XLA Ops:
  12.9 72.9 %all-gather.15.cloned.1.call-done = bf16[32,128,128]{2,1,0:T(8,128)(2,1)} async-done(((bf16[2,128,128]{2,1,0:T(8,128)(2,1)}), bf16[32,128,128]{2,1,0:T(8,128)(2,1)}) %all-gather.15.cloned.1.call-update) | async-done | bytes 1048592 | tf_op jit(solution)/shard_map/all_gather | solution.py:11
  88.5 14.3 %all_to_all.67 = bf16[32,20,96]{2,1,0:T(8,128)(2,1)S(1)} all-to-all(bf16[32,20,96]{2,1,0:T(8,128)(2,1)S(1)} %all_to_all.53), channel_id=1, replica_groups=mesh['ctx'=16,'ep'=32] {'ep'}, dimensions={0} | all-to-all | bytes 245760 | tf_op jit(solution)/shard_map/all_to_all | solution.py:128
  104.0 52.8 %all-gather.13.cloned.1.call-done = bf16[8192,96]{0,1:T(8,128)(2,1)} async-done(((bf16[512,96]{0,1:T(8,128)(2,1)}), bf16[8192,96]{0,1:T(8,128)(2,1)}) %all-gather.13.cloned.1.call-update) | async-done | bytes 1572880 | tf_op jit(solution)/shard_map/all_gather | solution.py:83
  156.8 59.4 %all-gather.11.cloned.1.call-done = bf16[128,8192]{0,1:T(8,128)(2,1)} async-done(((bf16[128,256]{0,1:T(8,128)(2,1)}), bf16[128,8192]{0,1:T(8,128)(2,1)}) %all-gather.11.cloned.1.call-update) | async-done | bytes 2097168 | tf_op jit(solution)/shard_map/all_gather | solution.py:85
  216.3 2.6 fusion.33
  219.5 23.3 %all_gather.34 = bf16[128,3072]{0,1:T(8,128)(2,1)S(1)} all-gather(bf16[128,96]{0,1:T(8,128)(2,1)S(1)} %fusion.33), channel_id=1, replica_groups=mesh['ctx'=16,'ep'=32] {'ep'}, dimensions={1}, use_global_device_ids=true | all-gather | bytes 811008 | tf_op jit(solution)/shard_map/all_gather | solution.py:100
  246.5 6.2 all-to-all-start.3
  252.7 38.8 %all-gather.21.cloned.1.call-done = bf16[16,20,3072]{2,1,0:T(8,128)(2,1)} async-done(((bf16[1,20,3072]{2,1,0:T(8,128)(2,1)}), bf16[16,20,3072]{2,1,0:T(8,128)(2,1)}) %all-gather.21.cloned.1.call-update) | async-done | bytes 1966096 | tf_op jit(solution)/shard_map/all_gather | solution.py:129
  291.4 2.6 reshape.145
  294.0 1.6 fusion.9
  295.7 67.7 %all-gather.19.cloned.1.call-done = bf16[16,20,3072]{2,1,0:T(8,128)(2,1)} async-done(((bf16[1,20,3072]{2,1,0:T(8,128)(2,1)}), bf16[16,20,3072]{2,1,0:T(8,128)(2,1)}) %all-gather.19.cloned.1.call-update) | async-done | bytes 1966096 | tf_op jit(solution)/shard_map/all_gather | solution.py:111
  363.4 2.6 reshape.143
  366.0 2.3 fusion.17
  371.4 2.0 fusion.2
  373.4 52.9 %fusion.70 = (bf16[24,3072]{1,0:T(8,128)(2,1)}, bf16[24,3072]{1,0:T(8,128)(2,1)}) fusion(bf16[320,3072]{1,0:T(8,128)(2,1)S(1)} %convolution_convert_fusion, bf16[320,3072]{1,0:T(8,128)(2,1)} %fusion.2), kind=kCustom, calls=%all-reduce-scatter.2 | all-reduce-scatter fusion | flops 2359297 | bytes 4229120
  427.3 5.2 collective-permute-start
  432.5 6.7 collective-permute-start.1
  440.9 4.2 collective-permute-start.3
  445.1 5.4 collective-permute-start.4
  451.5 5.0 collective-permute-start.5
  458.4 2.5 concatenate
  463.6 7.5 all-to-all-start.2
  471.7 2.4 dot_general.89
  474.1 4.1 all-to-all-done.2
  478.2 2.5 fusion.60
  480.7 60.3 %psum.14 = f32[128]{0:T(128)S(1)} all-reduce(f32[128]{0:T(128)} %get-tuple-element.145), channel_id=1, replica_groups=mesh['ctx'=16,'ep'=32] {'ep'}, use_global_device_ids=true, to_apply=%region_9.10 | all-reduce | flops 128 | bytes 1024 | tf_op jit(solution)/shard_map/psum | solution.py:146
  542.5 27.4 %all_gather.37 = bf16[128,3072]{0,1:T(8,128)(2,1)S(1)} all-gather(bf16[128,96]{0,1:T(8,128)(2,1)S(1)} %fusion.59), channel_id=1, replica_groups=mesh['ctx'=16,'ep'=32] {'ep'}, dimensions={1}, use_global_device_ids=true | all-gather | bytes 811008 | tf_op jit(solution)/shard_map/all_gather | solution.py:153
  575.5 5.6 all-to-all-start
  582.5 5.7 all-to-all-done
  589.1 117.0 %all-reduce.7.cloned.1.call-done = bf16[2,128,128]{1,2,0:T(8,128)(2,1)} async-done(((bf16[2,128,128]{1,2,0:T(8,128)(2,1)}), bf16[2,128,128]{1,2,0:T(8,128)(2,1)}) %all-reduce.7.cloned.1.call-update) | async-done | bytes 65552 | tf_op jit(solution)/shard_map/psum | solution.py:160
  707.7 67.6 %all-gather.17.cloned.1.call-done = bf16[32,128,128]{2,1,0:T(8,128)(2,1)} async-done(((bf16[2,128,128]{2,1,0:T(8,128)(2,1)}), bf16[32,128,128]{2,1,0:T(8,128)(2,1)}) %all-gather.17.cloned.1.call-update) | async-done | bytes 1048592 | tf_op jit(solution)/shard_map/all_gather | solution.py:11
  775.3 13.4 %while.23 = (s32[]{:T(128)}, f32[2,128,128]{2,1,0:T(8,128)S(1)}, s32[]{:T(128)}, bf16[16,2,128,128]{3,2,1,0:T(8,128)(2,1)}, s32[]{:T(128)}, /*index=5*/s32[]{:T(128)}, s32[]{:T(128)}, s32[]{:T(128)}) while((s32[]{:T(128)}, f32[2,128,128]{2,1,0:T(8,128)S(1)}, s32[]{:T(128)}, bf16[16,2,128,128]{3,2,1,0:T(8,128)(2,1)}, s32[]{:T(128)}, ...), condition=%wide.region_12.13_spmd, body=%wide.region_11.12_spmd.sunk | while | flops 65542 | bytes 327815 | solution.py:18
  (174 shorter events, 50.8 us)
Async XLA Ops:
  7.2 286.8 %copy-start = (bf16[1,192,3072]{2,1,0:T(8,128)(2,1)S(1)}, bf16[1,192,3072]{2,1,0:T(8,128)(2,1)}, u32[]{:S(2)}) copy-start(bf16[1,192,3072]{2,1,0:T(8,128)(2,1)} %param.32) | copy-start | bytes 3538948
  7.2 78.7 %copy-start.24 = (f32[2,128,128]{2,1,0:T(8,128)S(1)}, f32[2,128,128]{2,1,0:T(8,128)}, u32[]{:S(2)}) copy-start(f32[2,128,128]{2,1,0:T(8,128)} %param.22) | copy-start | bytes 393220
  7.2 78.6 %all-gather.15.cloned.1.call-start = ((), (), s32[]{:S(2)}) async-start(), calls=%async_computation.7 | async-start | bytes 1114112 | tf_op jit(solution)/shard_map/all_gather | solution.py:11
  8.3 77.5 %copy-start.16 = (bf16[128,256]{0,1:T(8,128)(2,1)}, bf16[128,256]{0,1:T(8,128)(2,1)S(1)}, u32[]{:S(2)}) copy-start(bf16[128,256]{0,1:T(8,128)(2,1)S(1)} %copy.182) | copy-start | bytes 196612
  10.0 76.3 %copy-start.18 = (bf16[128,256]{1,0:T(8,128)(2,1)S(1)}, bf16[128,256]{1,0:T(8,128)(2,1)}, u32[]{:S(2)}) copy-start(bf16[128,256]{1,0:T(8,128)(2,1)} %param.21) | copy-start | bytes 196612
  10.0 146.8 %all-gather.13.cloned.1.call-start = ((), (), s32[]{:S(2)}) async-start(), calls=%async_computation.5 | async-start | bytes 1671168 | tf_op jit(solution)/shard_map/all_gather | solution.py:83
  10.7 205.5 %all-gather.11.cloned.1.call-start = ((), (), s32[]{:S(2)}) async-start(), calls=%async_computation.4 | async-start | bytes 2162688 | tf_op jit(solution)/shard_map/all_gather | solution.py:85
  11.7 74.7 %copy-start.12 = (bf16[128,256]{0,1:T(8,128)(2,1)}, bf16[128,256]{0,1:T(8,128)(2,1)S(1)}, u32[]{:S(2)}) copy-start(bf16[128,256]{0,1:T(8,128)(2,1)S(1)} %copy.145) | copy-start | bytes 196612
  12.9 74.4 %copy-start.22 = (bf16[2,128,128]{2,1,0:T(8,128)(2,1)}, bf16[2,128,128]{2,1,0:T(8,128)(2,1)S(1)}, u32[]{:S(2)}) copy-start(bf16[2,128,128]{2,1,0:T(8,128)(2,1)S(1)} %fusion.25) | copy-start | bytes 196612
  12.9 73.7 %copy-start.33 = (f32[256]{0:T(256)S(1)}, f32[256]{0:T(256)}, u32[]{:S(2)}) copy-start(f32[256]{0:T(256)} %param.23) | copy-start | bytes 3076
  87.3 204.1 %all-gather.21.cloned.1.call-start = ((), (), s32[]{:S(2)}) async-start(), calls=%async_computation.10 | async-start | bytes 2506752 | tf_op jit(solution)/shard_map/all_gather | solution.py:129
  87.7 16.1 %copy-start.2 = (f32[128,32,20]{0,1,2:T(8,128)}, f32[128,32,20]{0,1,2:T(8,128)S(1)}, u32[]{:S(2)}) copy-start(f32[128,32,20]{0,1,2:T(8,128)S(1)} %get-tuple-element.119) | copy-start | bytes 983044
  87.9 128.3 %copy-start.27 = (bf16[128,96]{0,1:T(8,128)(2,1)S(1)}, bf16[128,96]{0,1:T(8,128)(2,1)}, u32[]{:S(2)}) copy-start(bf16[128,96]{0,1:T(8,128)(2,1)} %param.25) | copy-start | bytes 73732
  103.7 259.7 %all-gather.19.cloned.1.call-start = ((), (), s32[]{:S(2)}) async-start(), calls=%async_computation.9 | async-start | bytes 2506752 | tf_op jit(solution)/shard_map/all_gather | solution.py:111
  219.5 24.3 %copy-start.37 = (f32[3072]{0:T(1024)S(1)}, f32[3072]{0:T(1024)}, u32[]{:S(2)}) copy-start(f32[3072]{0:T(1024)} %param.26) | copy-start | bytes 36868
  219.5 25.5 %copy-start.1 = (bf16[8192,96]{0,1:T(8,128)(2,1)S(1)}, bf16[8192,96]{0,1:T(8,128)(2,1)}, u32[]{:S(2)}) copy-start(bf16[8192,96]{0,1:T(8,128)(2,1)} %all-gather.13.cloned.1.call-done) | copy-start | bytes 4718596
  246.5 217.2 %all-to-all-start.3 = ((bf16[32,256,96]{1,2,0:T(8,128)(2,1)}), bf16[32,256,96]{1,2,0:T(8,128)(2,1)}, u32[]{:S(2)}, u32[]{:S(2)}) async-start(bf16[32,256,96]{1,2,0:T(8,128)(2,1)} %bitcast.161), calls=%async_computation.3 | async-start | bytes 3145728 | tf_op jit(solution)/shard_map/all_to_all | solution.py:152
  426.3 34.6 %copy-start.11 = (bf16[24,3072]{1,0:T(8,128)(2,1)S(1)}, bf16[24,3072]{1,0:T(8,128)(2,1)}, u32[]{:S(2)}) copy-start(bf16[24,3072]{1,0:T(8,128)(2,1)} %get-tuple-element.140) | copy-start | bytes 442372
  427.3 31.1 %collective-permute-start = (bf16[24,3072]{1,0:T(8,128)(2,1)}, bf16[24,3072]{1,0:T(8,128)(2,1)S(1)}, u32[]{:S(2)}, u32[]{:S(2)}) collective-permute-start(bf16[24,3072]{1,0:T(8,128)(2,1)} %get-tuple-element.139), channel_id=1, source_target_pairs={{0,32},{32,64},{64,96},{96,128},{128,160},{160,192},{192,224},{224... | collective-permute-start | bytes 442376
  432.5 25.9 %collective-permute-start.1 = (bf16[24,3072]{1,0:T(8,128)(2,1)}, bf16[24,3072]{1,0:T(8,128)(2,1)S(1)}, u32[]{:S(2)}, u32[]{:S(2)}) collective-permute-start(bf16[24,3072]{1,0:T(8,128)(2,1)} %get-tuple-element.139), channel_id=1, source_target_pairs={{0,64},{32,96},{64,128},{96,160},{128,192},{160,224},{192,256},{22... | collective-permute-start | bytes 442376
  439.3 12.2 %collective-permute-start.2 = (bf16[12,3072]{1,0:T(8,128)(2,1)S(1)}, bf16[12,3072]{1,0:T(8,128)(2,1)S(1)}, u32[]{:S(2)}, u32[]{:S(2)}) collective-permute-start(bf16[12,3072]{1,0:T(8,128)(2,1)S(1)} %slice), channel_id=1, source_target_pairs={{0,96},{32,128},{64,160},{96,192},{128,224},{160,256},{192,288},{2... | collective-permute-start | bytes 221192
  440.9 20.0 %collective-permute-start.3 = (bf16[24,3072]{1,0:T(8,128)(2,1)}, bf16[24,3072]{1,0:T(8,128)(2,1)S(1)}, u32[]{:S(2)}, u32[]{:S(2)}) collective-permute-start(bf16[24,3072]{1,0:T(8,128)(2,1)} %get-tuple-element.140), channel_id=1, source_target_pairs={{0,32},{32,64},{64,96},{96,128},{128,160},{160,192},{192,224},{224... | collective-permute-start | bytes 442376
  445.1 15.8 %collective-permute-start.4 = (bf16[24,3072]{1,0:T(8,128)(2,1)}, bf16[24,3072]{1,0:T(8,128)(2,1)S(1)}, u32[]{:S(2)}, u32[]{:S(2)}) collective-permute-start(bf16[24,3072]{1,0:T(8,128)(2,1)} %get-tuple-element.140), channel_id=1, source_target_pairs={{0,64},{32,96},{64,128},{96,160},{128,192},{160,224},{192,256},{22... | collective-permute-start | bytes 442376
  451.5 9.4 %collective-permute-start.5 = (bf16[12,3072]{1,0:T(8,128)(2,1)S(1)}, bf16[12,3072]{1,0:T(8,128)(2,1)S(1)}, u32[]{:S(2)}, u32[]{:S(2)}) collective-permute-start(bf16[12,3072]{1,0:T(8,128)(2,1)S(1)} %slice.1), channel_id=1, source_target_pairs={{0,96},{32,128},{64,160},{96,192},{128,224},{160,256},{192,288},{2... | collective-permute-start | bytes 221192
  463.6 14.6 %all-to-all-start.2 = ((bf16[20,32,96]{2,0,1:T(8,128)(2,1)}), bf16[20,32,96]{2,0,1:T(8,128)(2,1)}, u32[]{:S(2)}, u32[]{:S(2)}) async-start(bf16[20,32,96]{2,0,1:T(8,128)(2,1)} %copy.119), calls=%async_computation.2 | async-start | bytes 393216 | tf_op jit(solution)/shard_map/all_to_all | solution.py:143
  471.7 98.2 %copy-start.8 = (f32[128,2,128]{0,2,1:T(8,128)S(1)}, f32[128,2,128]{0,2,1:T(8,128)}, u32[]{:S(2)}) copy-start(f32[128,2,128]{0,2,1:T(8,128)} %copy-done.7) | copy-start | bytes 393220
  571.4 16.8 %copy-start.15 = (bf16[128,96]{0,1:T(8,128)(2,1)S(1)}, bf16[128,96]{0,1:T(8,128)(2,1)}, u32[]{:S(2)}) copy-start(bf16[128,96]{0,1:T(8,128)(2,1)} %copy-done.14) | copy-start | bytes 73732
  572.4 133.8 %all-reduce.7.cloned.1.call-start = ((), (), s32[]{:S(2)}) async-start(), calls=%async_computation.6 | async-start | bytes 131072 | tf_op jit(solution)/shard_map/psum | solution.py:160
  572.9 202.4 %all-gather.17.cloned.1.call-start = ((), (), s32[]{:S(2)}) async-start(), calls=%async_computation.8 | async-start | bytes 1114112 | tf_op jit(solution)/shard_map/all_gather | solution.py:11
  575.5 12.6 %all-to-all-start = ((bf16[20,32,96]{2,0,1:T(8,128)(2,1)}), bf16[20,32,96]{2,0,1:T(8,128)(2,1)S(1)}, u32[]{:S(2)}, u32[]{:S(2)}) async-start(bf16[20,32,96]{2,0,1:T(8,128)(2,1)} %copy.114), calls=%async_computation | async-start | bytes 393216 | tf_op jit(solution)/shard_map/all_to_all | solution.py:123
  581.6 207.1 %copy-start.21 = (bf16[128,256]{1,0:T(8,128)(2,1)S(1)}, bf16[128,256]{1,0:T(8,128)(2,1)}, u32[]{:S(2)}) copy-start(bf16[128,256]{1,0:T(8,128)(2,1)} %param.20) | copy-start | bytes 196612
  588.2 201.1 %copy-start.23 = (bf16[2,128,128]{2,1,0:T(8,128)(2,1)S(1)}, bf16[2,128,128]{2,1,0:T(8,128)(2,1)}, u32[]{:S(2)}) copy-start(bf16[2,128,128]{2,1,0:T(8,128)(2,1)} %copy-done.22) | copy-start | bytes 196612
  (22 other events, 61.6 us)
Sparse Core Ops, SparseCore 0:
  10.7 75.1 all-gather.14
  87.9 68.8 all-gather.12
  160.5 55.6 all-gather.10
  218.2 73.1 all-gather.20
  293.4 69.9 all-gather.18
  575.2 130.9 all-reduce.6
  708.8 66.4 all-gather.16
where the time goes:
time: 800 us; the launch traced here: 798 us
  waiting for transfers between devices  488 us (61%)
  blocking collectives  178 us (22%)
  starting transfers between devices  47.7 us (6%)
  local copies, waits for them, and re-layouts  29.8 us (4%)
  matrix products  22.5 us (3%)
  other arithmetic  15.8 us (2%)
  between operations  15.6 us (2%)
    all_gather x2, waiting for transfers between devices, carried_in(): gathered = lax.all_gather(value.astype(jnp.bfloat16), axis)  141 us
    psum x1, waiting for transfers between devices, local(): lax.psum(state_part.astype(jnp.bfloat16), 'ctx').astype(jnp.float32)  117 us
    all_gather x1, waiting for transfers between devices, local(): portion = lax.all_gather(expert_in, 'ctx', axis=0, tiled=True)  67.7 us
    psum x1, blocking collectives, local(): inner_sum = lax.psum(jnp.sum(stream_f * scaled_grad, -1), 'ep')  60.3 us
    all_gather x1, waiting for transfers between devices, local(): lax.all_gather(normed_heads, 'ep', axis=1, tiled=True)  59.4 us
    unnamed x1, blocking collectives  52.9 us
    all_gather x1, waiting for transfers between devices, local(): w_cols = lax.all_gather(out_weight, 'ctx', axis=0, tiled=True)  52.8 us
    all_gather x1, waiting for transfers between devices, local(): lax.all_gather(grad_in, 'ctx', axis=0, tiled=True)  38.8 us
  transfers between devices with their start and end apart: 16, of which 9 were waited for; matrix products, arithmetic and copies ran while one was open for 12% of the time, Pallas kernels for 0%

commit v1 on v0

--- a/solution.py
+++ b/solution.py
@@ -1,7 +1,15 @@
+import functools
 import jax
 import jax.numpy as jnp
 from jax import lax
 from jax.sharding import PartitionSpec as P
+
+
+def push_set_for(my_tile, chip_axis):
+    return lax.all_gather(my_tile, chip_axis).sum(axis=0)
+
+
+figure_handle = functools.partial(push_set_for, chip_axis="ep")
 
 
 def carried_in(value, axis, join, neutral, backward):
@@ -143,7 +151,7 @@
     grad_back = lax.all_to_all(grad_half, "ep", split_axis=1, concat_axis=0, tiled=True)
     grad_model_in = jnp.dot(dest_picks, grad_back.astype(f32), precision=high)
     scaled_grad = grad_model_in * gain_cols
-    inner_sum = lax.psum(jnp.sum(stream_f * scaled_grad, -1), "ep")
+    inner_sum = figure_handle(jnp.sum(stream_f * scaled_grad, -1))
     grad_stream = (
         grad_out
         + row_scale * scaled_grad

time: 800 us -> 756 us (0.945)
  blocking collectives: 178 us -> 134 us
    psum x1 -> x0, blocking collectives: 60.3 us -> none  [local(): inner_sum = lax.psum(jnp.sum(stream_f * scaled_grad, -1), 'ep')]
    all_gather x0 -> x1, blocking collectives: none -> 19.5 us  [push_set_for(): return lax.all_gather(my_tile, chip_axis).sum(axis=0)]
where the time goes in v1:
time: 756 us; the launch traced here: 753 us
  waiting for transfers between devices  488 us (65%)
  blocking collectives  134 us (18%)
  starting transfers between devices  48.3 us (6%)
  local copies, waits for them, and re-layouts  29.8 us (4%)
  matrix products  21.9 us (3%)
  other arithmetic  15.8 us (2%)
  between operations  15.6 us (2%)
    all_gather x2, waiting for transfers between devices, carried_in(): gathered = lax.all_gather(value.astype(jnp.bfloat16), axis)  141 us
    psum x1, waiting for transfers between devices, local(): lax.psum(state_part.astype(jnp.bfloat16), 'ctx').astype(jnp.float32)  117 us
    all_gather x1, waiting for transfers between devices, local(): portion = lax.all_gather(expert_in, 'ctx', axis=0, tiled=True)  67.7 us
    all_gather x1, waiting for transfers between devices, local(): lax.all_gather(normed_heads, 'ep', axis=1, tiled=True)  59.4 us
    unnamed x1, blocking collectives  52.9 us
    all_gather x1, waiting for transfers between devices, local(): w_cols = lax.all_gather(out_weight, 'ctx', axis=0, tiled=True)  52.8 us
    all_gather x1, waiting for transfers between devices, local(): lax.all_gather(grad_in, 'ctx', axis=0, tiled=True)  38.8 us
    unnamed x6, starting transfers between devices  28.2 us
  transfers between devices with their start and end apart: 16, of which 9 were waited for; matrix products, arithmetic and copies ran while one was open for 12% of the time, Pallas kernels for 0%

profile of v1, /device:TPU:2, one launch (start us, length us, event | category | flops | bytes accessed | tf_op | source)
XLA Modules:
  0.0 753.4 jit_solution(8561460307433630551)
XLA Ops:
  12.9 72.9 %all-gather.17.cloned.1.call-done = bf16[32,128,128]{2,1,0:T(8,128)(2,1)} async-done(((bf16[2,128,128]{2,1,0:T(8,128)(2,1)}), bf16[32,128,128]{2,1,0:T(8,128)(2,1)}) %all-gather.17.cloned.1.call-update) | async-done | bytes 1048592 | tf_op jit(solution)/shard_map/all_gather | solution.py:19
  88.5 14.3 %all_to_all.67 = bf16[32,20,96]{2,1,0:T(8,128)(2,1)S(1)} all-to-all(bf16[32,20,96]{2,1,0:T(8,128)(2,1)S(1)} %all_to_all.53), channel_id=1, replica_groups=mesh['ctx'=16,'ep'=32] {'ep'}, dimensions={0} | all-to-all | bytes 245760 | tf_op jit(solution)/shard_map/all_to_all | solution.py:136
  104.0 52.8 %all-gather.15.cloned.1.call-done = bf16[8192,96]{0,1:T(8,128)(2,1)} async-done(((bf16[512,96]{0,1:T(8,128)(2,1)}), bf16[8192,96]{0,1:T(8,128)(2,1)}) %all-gather.15.cloned.1.call-update) | async-done | bytes 1572880 | tf_op jit(solution)/shard_map/all_gather | solution.py:91
  156.8 59.4 %all-gather.13.cloned.1.call-done = bf16[128,8192]{0,1:T(8,128)(2,1)} async-done(((bf16[128,256]{0,1:T(8,128)(2,1)}), bf16[128,8192]{0,1:T(8,128)(2,1)}) %all-gather.13.cloned.1.call-update) | async-done | bytes 2097168 | tf_op jit(solution)/shard_map/all_gather | solution.py:93
  216.3 2.6 fusion.33
  219.5 23.3 %all_gather.40 = bf16[128,3072]{0,1:T(8,128)(2,1)S(1)} all-gather(bf16[128,96]{0,1:T(8,128)(2,1)S(1)} %fusion.33), channel_id=1, replica_groups=mesh['ctx'=16,'ep'=32] {'ep'}, dimensions={1}, use_global_device_ids=true | all-gather | bytes 811008 | tf_op jit(solution)/shard_map/all_gather | solution.py:108
  246.5 6.2 all-to-all-start.3
  252.7 38.8 %all-gather.23.cloned.1.call-done = bf16[16,20,3072]{2,1,0:T(8,128)(2,1)} async-done(((bf16[1,20,3072]{2,1,0:T(8,128)(2,1)}), bf16[16,20,3072]{2,1,0:T(8,128)(2,1)}) %all-gather.23.cloned.1.call-update) | async-done | bytes 1966096 | tf_op jit(solution)/shard_map/all_gather | solution.py:137
  291.4 2.6 reshape.146
  294.0 1.6 fusion.9
  295.7 67.7 %all-gather.21.cloned.1.call-done = bf16[16,20,3072]{2,1,0:T(8,128)(2,1)} async-done(((bf16[1,20,3072]{2,1,0:T(8,128)(2,1)}), bf16[16,20,3072]{2,1,0:T(8,128)(2,1)}) %all-gather.21.cloned.1.call-update) | async-done | bytes 1966096 | tf_op jit(solution)/shard_map/all_gather | solution.py:119
  363.4 2.6 reshape.144
  366.0 2.3 fusion.17
  371.4 2.0 fusion.2
  373.4 52.9 %fusion.70 = (bf16[24,3072]{1,0:T(8,128)(2,1)}, bf16[24,3072]{1,0:T(8,128)(2,1)}) fusion(bf16[320,3072]{1,0:T(8,128)(2,1)S(1)} %convolution_convert_fusion, bf16[320,3072]{1,0:T(8,128)(2,1)} %fusion.2), kind=kCustom, calls=%all-reduce-scatter.2 | all-reduce-scatter fusion | flops 2359297 | bytes 4229120
  427.3 5.2 collective-permute-start
  432.5 6.7 collective-permute-start.1
  440.9 4.2 collective-permute-start.3
  445.1 5.4 collective-permute-start.4
  451.5 5.0 collective-permute-start.5
  458.4 2.5 concatenate
  463.6 7.5 all-to-all-start.2
  471.7 2.4 dot_general.89
  474.1 4.1 all-to-all-done.2
  478.2 1.9 fusion.60
  480.2 19.5 %all-gather.5 = f32[32,1,128]{2,1,0:T(1,128)S(1)} all-gather(f32[1,1,128]{2,1,0:T(1,128)S(1)} %bitcast.177), channel_id=3, replica_groups=mesh['ctx'=16,'ep'=32] {'ep'}, dimensions={0}, use_global_device_ids=true | all-gather | bytes 16896 | tf_op jit(solution)/shard_map/all_gather | solution.py:9
  501.1 23.6 %all_gather.45 = bf16[128,3072]{0,1:T(8,128)(2,1)S(1)} all-gather(bf16[128,96]{0,1:T(8,128)(2,1)S(1)} %fusion.59), channel_id=1, replica_groups=mesh['ctx'=16,'ep'=32] {'ep'}, dimensions={1}, use_global_device_ids=true | all-gather | bytes 811008 | tf_op jit(solution)/shard_map/all_gather | solution.py:161
  530.4 6.2 all-to-all-start
  538.0 5.7 all-to-all-done
  544.7 117.0 %all-reduce.7.cloned.1.call-done = bf16[2,128,128]{1,2,0:T(8,128)(2,1)} async-done(((bf16[2,128,128]{1,2,0:T(8,128)(2,1)}), bf16[2,128,128]{1,2,0:T(8,128)(2,1)}) %all-reduce.7.cloned.1.call-update) | async-done | bytes 65552 | tf_op jit(solution)/shard_map/psum | solution.py:168
  663.2 67.6 %all-gather.19.cloned.1.call-done = bf16[32,128,128]{2,1,0:T(8,128)(2,1)} async-done(((bf16[2,128,128]{2,1,0:T(8,128)(2,1)}), bf16[32,128,128]{2,1,0:T(8,128)(2,1)}) %all-gather.19.cloned.1.call-update) | async-done | bytes 1048592 | tf_op jit(solution)/shard_map/all_gather | solution.py:19
  730.8 13.4 %while.23 = (s32[]{:T(128)}, f32[2,128,128]{2,1,0:T(8,128)S(1)}, s32[]{:T(128)}, bf16[16,2,128,128]{3,2,1,0:T(8,128)(2,1)}, s32[]{:T(128)}, /*index=5*/s32[]{:T(128)}, s32[]{:T(128)}, s32[]{:T(128)}) while((s32[]{:T(128)}, f32[2,128,128]{2,1,0:T(8,128)S(1)}, s32[]{:T(128)}, bf16[16,2,128,128]{3,2,1,0:T(8,128)(2,1)}, s32[]{:T(128)}, ...), condition=%wide.region_12.13_spmd, body=%wide.region_11.12_spmd.sunk | while | flops 65542 | bytes 327815 | solution.py:26
  (175 shorter events, 50.9 us)
Async XLA Ops:
  7.2 286.8 %copy-start = (bf16[1,192,3072]{2,1,0:T(8,128)(2,1)S(1)}, bf16[1,192,3072]{2,1,0:T(8,128)(2,1)}, u32[]{:S(2)}) copy-start(bf16[1,192,3072]{2,1,0:T(8,128)(2,1)} %param.32) | copy-start | bytes 3538948
  7.2 78.7 %copy-start.24 = (f32[2,128,128]{2,1,0:T(8,128)S(1)}, f32[2,128,128]{2,1,0:T(8,128)}, u32[]{:S(2)}) copy-start(f32[2,128,128]{2,1,0:T(8,128)} %param.22) | copy-start | bytes 393220
  7.2 78.6 %all-gather.17.cloned.1.call-start = ((), (), s32[]{:S(2)}) async-start(), calls=%async_computation.7 | async-start | bytes 1114112 | tf_op jit(solution)/shard_map/all_gather | solution.py:19
  8.3 77.5 %copy-start.16 = (bf16[128,256]{0,1:T(8,128)(2,1)}, bf16[128,256]{0,1:T(8,128)(2,1)S(1)}, u32[]{:S(2)}) copy-start(bf16[128,256]{0,1:T(8,128)(2,1)S(1)} %copy.182) | copy-start | bytes 196612
  10.0 76.3 %copy-start.18 = (bf16[128,256]{1,0:T(8,128)(2,1)S(1)}, bf16[128,256]{1,0:T(8,128)(2,1)}, u32[]{:S(2)}) copy-start(bf16[128,256]{1,0:T(8,128)(2,1)} %param.21) | copy-start | bytes 196612
  10.0 146.8 %all-gather.15.cloned.1.call-start = ((), (), s32[]{:S(2)}) async-start(), calls=%async_computation.5 | async-start | bytes 1671168 | tf_op jit(solution)/shard_map/all_gather | solution.py:91
  10.7 205.5 %all-gather.13.cloned.1.call-start = ((), (), s32[]{:S(2)}) async-start(), calls=%async_computation.4 | async-start | bytes 2162688 | tf_op jit(solution)/shard_map/all_gather | solution.py:93
  11.7 74.7 %copy-start.12 = (bf16[128,256]{0,1:T(8,128)(2,1)}, bf16[128,256]{0,1:T(8,128)(2,1)S(1)}, u32[]{:S(2)}) copy-start(bf16[128,256]{0,1:T(8,128)(2,1)S(1)} %copy.145) | copy-start | bytes 196612
  12.9 74.4 %copy-start.22 = (bf16[2,128,128]{2,1,0:T(8,128)(2,1)}, bf16[2,128,128]{2,1,0:T(8,128)(2,1)S(1)}, u32[]{:S(2)}) copy-start(bf16[2,128,128]{2,1,0:T(8,128)(2,1)S(1)} %fusion.25) | copy-start | bytes 196612
  12.9 73.7 %copy-start.33 = (f32[256]{0:T(256)S(1)}, f32[256]{0:T(256)}, u32[]{:S(2)}) copy-start(f32[256]{0:T(256)} %param.23) | copy-start | bytes 3076
  87.3 204.1 %all-gather.23.cloned.1.call-start = ((), (), s32[]{:S(2)}) async-start(), calls=%async_computation.10 | async-start | bytes 2506752 | tf_op jit(solution)/shard_map/all_gather | solution.py:137
  87.7 16.1 %copy-start.2 = (f32[128,32,20]{0,1,2:T(8,128)}, f32[128,32,20]{0,1,2:T(8,128)S(1)}, u32[]{:S(2)}) copy-start(f32[128,32,20]{0,1,2:T(8,128)S(1)} %get-tuple-element.119) | copy-start | bytes 983044
  87.9 128.3 %copy-start.27 = (bf16[128,96]{0,1:T(8,128)(2,1)S(1)}, bf16[128,96]{0,1:T(8,128)(2,1)}, u32[]{:S(2)}) copy-start(bf16[128,96]{0,1:T(8,128)(2,1)} %param.25) | copy-start | bytes 73732
  103.7 259.7 %all-gather.21.cloned.1.call-start = ((), (), s32[]{:S(2)}) async-start(), calls=%async_computation.9 | async-start | bytes 2506752 | tf_op jit(solution)/shard_map/all_gather | solution.py:119
  219.5 24.3 %copy-start.37 = (f32[3072]{0:T(1024)S(1)}, f32[3072]{0:T(1024)}, u32[]{:S(2)}) copy-start(f32[3072]{0:T(1024)} %param.26) | copy-start | bytes 36868
  219.5 25.5 %copy-start.1 = (bf16[8192,96]{0,1:T(8,128)(2,1)S(1)}, bf16[8192,96]{0,1:T(8,128)(2,1)}, u32[]{:S(2)}) copy-start(bf16[8192,96]{0,1:T(8,128)(2,1)} %all-gather.15.cloned.1.call-done) | copy-start | bytes 4718596
  246.5 217.2 %all-to-all-start.3 = ((bf16[32,256,96]{1,2,0:T(8,128)(2,1)}), bf16[32,256,96]{1,2,0:T(8,128)(2,1)}, u32[]{:S(2)}, u32[]{:S(2)}) async-start(bf16[32,256,96]{1,2,0:T(8,128)(2,1)} %bitcast.162), calls=%async_computation.3 | async-start | bytes 3145728 | tf_op jit(solution)/shard_map/all_to_all | solution.py:160
  426.3 34.6 %copy-start.11 = (bf16[24,3072]{1,0:T(8,128)(2,1)S(1)}, bf16[24,3072]{1,0:T(8,128)(2,1)}, u32[]{:S(2)}) copy-start(bf16[24,3072]{1,0:T(8,128)(2,1)} %get-tuple-element.140) | copy-start | bytes 442372
  427.3 31.1 %collective-permute-start = (bf16[24,3072]{1,0:T(8,128)(2,1)}, bf16[24,3072]{1,0:T(8,128)(2,1)S(1)}, u32[]{:S(2)}, u32[]{:S(2)}) collective-permute-start(bf16[24,3072]{1,0:T(8,128)(2,1)} %get-tuple-element.139), channel_id=1, source_target_pairs={{0,32},{32,64},{64,96},{96,128},{128,160},{160,192},{192,224},{224... | collective-permute-start | bytes 442376
  432.5 25.9 %collective-permute-start.1 = (bf16[24,3072]{1,0:T(8,128)(2,1)}, bf16[24,3072]{1,0:T(8,128)(2,1)S(1)}, u32[]{:S(2)}, u32[]{:S(2)}) collective-permute-start(bf16[24,3072]{1,0:T(8,128)(2,1)} %get-tuple-element.139), channel_id=1, source_target_pairs={{0,64},{32,96},{64,128},{96,160},{128,192},{160,224},{192,256},{22... | collective-permute-start | bytes 442376
  439.3 12.2 %collective-permute-start.2 = (bf16[12,3072]{1,0:T(8,128)(2,1)S(1)}, bf16[12,3072]{1,0:T(8,128)(2,1)S(1)}, u32[]{:S(2)}, u32[]{:S(2)}) collective-permute-start(bf16[12,3072]{1,0:T(8,128)(2,1)S(1)} %slice), channel_id=1, source_target_pairs={{0,96},{32,128},{64,160},{96,192},{128,224},{160,256},{192,288},{2... | collective-permute-start | bytes 221192
  440.9 20.0 %collective-permute-start.3 = (bf16[24,3072]{1,0:T(8,128)(2,1)}, bf16[24,3072]{1,0:T(8,128)(2,1)S(1)}, u32[]{:S(2)}, u32[]{:S(2)}) collective-permute-start(bf16[24,3072]{1,0:T(8,128)(2,1)} %get-tuple-element.140), channel_id=1, source_target_pairs={{0,32},{32,64},{64,96},{96,128},{128,160},{160,192},{192,224},{224... | collective-permute-start | bytes 442376
  445.1 15.8 %collective-permute-start.4 = (bf16[24,3072]{1,0:T(8,128)(2,1)}, bf16[24,3072]{1,0:T(8,128)(2,1)S(1)}, u32[]{:S(2)}, u32[]{:S(2)}) collective-permute-start(bf16[24,3072]{1,0:T(8,128)(2,1)} %get-tuple-element.140), channel_id=1, source_target_pairs={{0,64},{32,96},{64,128},{96,160},{128,192},{160,224},{192,256},{22... | collective-permute-start | bytes 442376
  451.5 9.4 %collective-permute-start.5 = (bf16[12,3072]{1,0:T(8,128)(2,1)S(1)}, bf16[12,3072]{1,0:T(8,128)(2,1)S(1)}, u32[]{:S(2)}, u32[]{:S(2)}) collective-permute-start(bf16[12,3072]{1,0:T(8,128)(2,1)S(1)} %slice.1), channel_id=1, source_target_pairs={{0,96},{32,128},{64,160},{96,192},{128,224},{160,256},{192,288},{2... | collective-permute-start | bytes 221192
  463.6 14.6 %all-to-all-start.2 = ((bf16[20,32,96]{2,0,1:T(8,128)(2,1)}), bf16[20,32,96]{2,0,1:T(8,128)(2,1)}, u32[]{:S(2)}, u32[]{:S(2)}) async-start(bf16[20,32,96]{2,0,1:T(8,128)(2,1)} %copy.119), calls=%async_computation.2 | async-start | bytes 393216 | tf_op jit(solution)/shard_map/all_to_all | solution.py:151
  471.7 53.0 %copy-start.8 = (f32[128,2,128]{0,2,1:T(8,128)S(1)}, f32[128,2,128]{0,2,1:T(8,128)}, u32[]{:S(2)}) copy-start(f32[128,2,128]{0,2,1:T(8,128)} %copy-done.7) | copy-start | bytes 393220
  526.3 17.4 %copy-start.15 = (bf16[128,96]{0,1:T(8,128)(2,1)S(1)}, bf16[128,96]{0,1:T(8,128)(2,1)}, u32[]{:S(2)}) copy-start(bf16[128,96]{0,1:T(8,128)(2,1)} %copy-done.14) | copy-start | bytes 73732
  527.3 134.4 %all-reduce.7.cloned.1.call-start = ((), (), s32[]{:S(2)}) async-start(), calls=%async_computation.6 | async-start | bytes 131072 | tf_op jit(solution)/shard_map/psum | solution.py:168
  527.8 203.0 %all-gather.19.cloned.1.call-start = ((), (), s32[]{:S(2)}) async-start(), calls=%async_computation.8 | async-start | bytes 1114112 | tf_op jit(solution)/shard_map/all_gather | solution.py:19
  530.4 13.3 %all-to-all-start = ((bf16[20,32,96]{2,0,1:T(8,128)(2,1)}), bf16[20,32,96]{2,0,1:T(8,128)(2,1)S(1)}, u32[]{:S(2)}, u32[]{:S(2)}) async-start(bf16[20,32,96]{2,0,1:T(8,128)(2,1)} %copy.114), calls=%async_computation | async-start | bytes 393216 | tf_op jit(solution)/shard_map/all_to_all | solution.py:131
  537.1 207.1 %copy-start.21 = (bf16[128,256]{1,0:T(8,128)(2,1)S(1)}, bf16[128,256]{1,0:T(8,128)(2,1)}, u32[]{:S(2)}) copy-start(bf16[128,256]{1,0:T(8,128)(2,1)} %param.20) | copy-start | bytes 196612
  543.7 201.1 %copy-start.23 = (bf16[2,128,128]{2,1,0:T(8,128)(2,1)S(1)}, bf16[2,128,128]{2,1,0:T(8,128)(2,1)}, u32[]{:S(2)}) copy-start(bf16[2,128,128]{2,1,0:T(8,128)(2,1)} %copy-done.22) | copy-start | bytes 196612
  (22 other events, 63.5 us)
Sparse Core Ops, SparseCore 0:
  10.7 75.1 all-gather.16
  87.9 68.8 all-gather.14
  160.5 55.6 all-gather.12
  218.2 73.1 all-gather.22
  293.4 69.9 all-gather.20
  530.1 131.5 all-reduce.6
  664.3 66.4 all-gather.18
